TPU v7x, 256 devices: a whole 4x4x8 slice. The times are simulated.
256 devices in a mesh: shard: 64 (over y, z, core), cent: 4 (over x).
Axes of the slice: x: 4, y: 4, z: 8, core: 2. Of those that a mesh axis runs over, the one named last changes fastest.
Arguments:
- queries: bfloat16 [1024, 32, 128], P('shard'), may hold values from -6 to 6
- centroids: bfloat16 [196608, 128], P(('shard', 'cent')), may hold values from -0.5 to 0.5
- passages: bfloat16 [16384, 128, 128], P('shard', 'cent'), may hold values from -0.5 to 0.5
- lengths: int32 [16384], P('shard'), may hold values from 16 to 128, as said below
- passage_row: int32 [16384], replicated, may hold values from 0 to 16383, as said below
- candidates: int32 [1024, 16], P('shard'), may hold values from 0 to 16383, as said below
Outputs:
- token_best: float32 [1024, 32], P('shard')
- scores: float32 [1024, 16], P('shard')
Inputs may be any that keep to these rules, and one draw needn't show every extreme that they name: A permutation: passage g is stored at row passage_row[g]. The rows j < lengths[r] of stored passage r are real, the rest padding; the first stored passage of every index of shard has all 128. Among the 256 pairs of the queries of one index of shard, at most 12 have candidates stored at one owner (owner = passage_row[id] // 256); one owner takes exactly 12 pairs from every index of shard.
All inputs are finite; a program needn't handle non-finite values.
Results may differ from a plain program's by a relative error of at most 0.0003.
Values may be sent and summed in bfloat16 or wider, within the bound.
No kernel may reach another device: no remote copies, remote signals or barrier semaphores. Data moves between devices by JAX's collectives and lax.ppermute only.
A program may use at most 128 MiB of HBM per device.

v0:
```python
import jax
import jax.numpy as jnp
from jax import lax
from jax.sharding import PartitionSpec as P

masked_score = -1e30


def per_device(queries, centroids, passages, lengths, passage_row, candidates):
    query_count = queries.shape[0]
    query_tokens = queries.shape[1]
    feature_width = queries.shape[2]
    per_query = candidates.shape[1]
    passage_count = passages.shape[0]
    token_rows = passages.shape[1]
    shard_total = lax.axis_size("shard")
    capacity = max(2, 3 * query_count * per_query // shard_total)
    pairs_here = query_count * per_query
    my_shard = lax.axis_index("shard")
    query_block = lax.all_gather(queries, "shard", axis=0, tiled=True)
    cand_block = lax.all_gather(candidates, "shard", axis=0, tiled=True)
    flattened = query_block.reshape(-1, feature_width)
    scored = jnp.einsum("rd,cd->rc", flattened, centroids, preferred_element_type=jnp.float32)
    local_best = jnp.max(scored, axis=1).reshape(shard_total, query_count, query_tokens)
    gathered_best = lax.all_to_all(local_best, "shard", split_axis=0, concat_axis=0, tiled=True)
    shard_best = jnp.max(gathered_best, axis=0)
    all_rows = jnp.take(passage_row, cand_block.reshape(-1), axis=0)
    is_mine = (all_rows // passage_count == my_shard).reshape(shard_total, pairs_here)
    mine_int = is_mine.astype(jnp.int32)
    rank = jnp.cumsum(mine_int, axis=1) - mine_int
    source_ids = jnp.arange(shard_total, dtype=jnp.int32)[:, None]
    places = jnp.where(is_mine, source_ids * capacity + rank, shard_total * capacity).reshape(-1)
    pair_query = jnp.arange(shard_total * pairs_here, dtype=jnp.int32) // per_query
    slot_table = (
        jnp.zeros((shard_total * capacity,), jnp.int32)
        .at[places]
        .set(all_rows % passage_count, mode="drop")
    )
    query_table = (
        jnp.zeros((shard_total * capacity,), jnp.int32).at[places].set(pair_query, mode="drop")
    )
    asked = jnp.take(query_block, query_table, axis=0)
    chosen = jnp.take(passages, slot_table, axis=0)
    pair_scored = jnp.einsum("ntd,npd->ntp", asked, chosen, preferred_element_type=jnp.float32)
    token_index = lax.axis_index("cent") * token_rows + jnp.arange(token_rows, dtype=jnp.int32)
    valid_tokens = token_index[None, :] < jnp.take(lengths, slot_table, axis=0)[:, None]
    pair_scored = jnp.where(valid_tokens[:, None, :], pair_scored, masked_score)
    partial_value = jnp.max(pair_scored, axis=2)
    merged = lax.pmax(jnp.concatenate([shard_best, partial_value], axis=0), "cent")
    token_best = merged[:query_count]
    complete = merged[query_count:]
    pair_scores = (jnp.sum(complete, axis=1) / query_tokens).reshape(shard_total, capacity)
    returned = lax.all_to_all(pair_scores, "shard", split_axis=0, concat_axis=0, tiled=True)
    pair_rows = jnp.take(passage_row, candidates.reshape(-1), axis=0)
    owners = pair_rows // passage_count
    onehot = (owners[:, None] == jnp.arange(shard_total, dtype=jnp.int32)[None, :]).astype(
        jnp.int32
    )
    ranking = jnp.sum((jnp.cumsum(onehot, axis=0) - onehot) * onehot, axis=1)
    my_places = owners * capacity + ranking
    scores = jnp.take(returned.reshape(-1), my_places, axis=0).reshape(query_count, per_query)
    return (token_best, scores)


def solution(mesh):
    in_specs = (
        P("shard", None, None),
        P(("shard", "cent"), None),
        P("shard", "cent", None),
        P("shard"),
        P(),
        P("shard", None),
    )
    out_specs = (P("shard", None), P("shard", None))
    return jax.shard_map(
        per_device, mesh=mesh, in_specs=in_specs, out_specs=out_specs, check_vma=False
    )
```

profile of v0, /device:TPU:1, one launch (start us, length us, event | category | flops | bytes accessed | tf_op | source)
XLA Modules:
  0.0 415.2 jit_solution(12105765791642082866)
XLA Ops:
  7.2 0.0 copy-start
  7.2 0.0 copy-start.1
  7.2 0.0 all-gather.2.cloned.1.call-start
  7.2 0.7 all-gather.2.cloned.1.call-update
  7.9 0.8 reshape.445
  8.7 0.8 reshape.447
  9.5 0.8 reshape.446
  10.3 55.1 %all_gather.7 = s32[1024,16]{1,0:T(8,128)S(1)} all-gather(s32[16,16]{1,0:T(8,128)} %param.11), channel_id=1, replica_groups=mesh['shard'=64,'cent'=4] {'shard'}, dimensions={0}, use_global_device_ids=true | all-gather | bytes 66560 | tf_op jit(solution)/shard_map/all_gather | solution.py:21
  65.3 0.2 reshape.441
  65.6 0.2 reshape.444
  65.8 0.2 reshape.442
  66.0 2.1 gather_fusion.4
  68.1 0.6 reduce-window.16
  68.8 0.2 slice_reduce_fusion.1
  69.0 0.1 broadcast_bitcast_fusion
  69.1 0.1 copy.37
  69.1 0.1 compare_select_fusion.1
  69.2 0.0 copy-start.2
  69.3 90.5 %gather_fusion = s32[16384]{0:T(1024)S(1)} fusion(s32[16384]{0:T(1024)S(1)} %copy-done.1, s32[16384]{0:T(1024)S(1)} %broadcast_clamp_fusion), kind=kCustom, calls=%fused_computation | custom fusion | bytes 196608 | tf_op jit(solution)/shard_map/jit(_take)/gather | solution.py:27
  159.8 0.1 fusion.23
  159.9 0.6 reduce-window.14
  160.5 0.2 slice_reduce_fusion.2
  160.7 0.1 broadcast_add_fusion
  160.8 0.1 copy.30
  160.9 0.5 compare_select_fusion
  161.5 60.3 %scatter_custom_fusion.1 = s32[768]{0:T(1024)S(1)} fusion(s32[16384]{0:T(1024)S(1)} %bitcast.49, s32[16384]{0:T(1024)S(1)} %add_select_fusion, s32[]{:T(128)} %constant.143.clone.1), kind=kCustom, calls=%fused_computation.97 | custom fusion | bytes 3076 | tf_op jit(solution)/shard_map/scatter | solution.py:40
  221.8 60.5 %scatter_custom_fusion = s32[768]{0:T(1024)S(1)} fusion(s32[16384]{0:T(1024)S(1)} %bitcast.50, s32[16384]{0:T(1024)S(1)} %add_select_fusion.1, s32[]{:T(128)} %constant.143.clone.1), kind=kCustom, calls=%fused_computation.99 | custom fusion | bytes 3076 | tf_op jit(solution)/shard_map/scatter | solution.py:37
  282.3 5.0 %gather_fusion.1 = s32[768]{0:T(1024)S(1)} fusion(s32[256]{0:T(256)S(1)} %copy-done.2, s32[1024]{0:T(1024)S(1)} %pad_clamp_fusion.3), kind=kCustom, calls=%fused_computation.1 | custom fusion | bytes 9216 | tf_op jit(solution)/shard_map/jit(_take)/gather | solution.py:46
  287.3 0.0 slice-start
  287.4 0.0 copy-start.5
  287.4 4.5 %gather_fusion.3 = bf16[768,32,128]{2,1,0:T(8,128)(2,1)} fusion(bf16[256,32,128]{2,1,0:T(8,128)(2,1)S(1)} %copy-done, s32[1024]{0:T(1024)S(1)} %pad_clamp_fusion.3), kind=kCustom, calls=%fused_computation.3 | custom fusion | bytes 12585984 | tf_op jit(solution)/shard_map/jit(_take)/gather | solution.py:43
  291.9 0.1 fusion.19
  292.0 0.2 broadcast_compare_fusion
  292.2 0.0 all-gather.2.cloned.1.call-done
  292.3 17.0 %convolution_reduce_fusion = f32[32768]{0:T(1024)S(1)} fusion(bf16[32768,128]{1,0:T(8,128)(2,1)} %bitcast.43, bf16[768,128]{1,0:T(8,128)(2,1)S(1)} %copy-done.5), kind=kOutput, calls=%fused_computation.8 | convolution fusion | flops 6467584000 | bytes 8716288 | tf_op jit(solution)/shard_map/rd,cd->rc/dot_general | solution.py:23
  309.3 0.2 reshape.440
  309.5 0.9 reshape.532
  310.4 6.4 %all-to-all-start = ((f32[64,1,512]{2,1,0:T(1,128)}), f32[64,1,512]{2,1,0:T(1,128)S(1)}, u32[]{:S(2)}, u32[]{:S(2)}) async-start(f32[64,1,512]{2,1,0:T(1,128)} %reshape.532), calls=%async_computation | async-start | bytes 262144 | tf_op jit(solution)/shard_map/all_to_all | solution.py:25
  316.8 0.0 all-reduce.2.cloned.1.call-start
  316.9 8.3 %gather_fusion.2 = bf16[768,32,128]{2,1,0:T(8,128)(2,1)} fusion(bf16[1024,32,128]{2,1,0:T(8,128)(2,1)} %all-gather.2.cloned.1.call-done, s32[1024]{0:T(1024)S(1)} %pad_clamp_fusion.2), kind=kCustom, calls=%fused_computation.2 | custom fusion | bytes 12585984 | tf_op jit(solution)/shard_map/jit(_take)/gather | solution.py:42
  325.2 8.3 %select_reduce_fusion = f32[768,32]{1,0:T(8,128)S(1)} fusion(pred[768,32]{1,0:T(8,128)(4,1)S(1)} %broadcast_compare_fusion, bf16[768,32,128]{2,1,0:T(8,128)(2,1)} %gather_fusion.3, pred[768]{0:T(1024)(128)(4,1)S(1)} %get-tuple-element.9, bf16[768,32,128]{2,1,0:T(8,128)(2,1)} %gather_fusion.2, pred[768]{0:T(1024)(128)(4,1)S(1)} %compare_and_fusion), kind=kOutput, calls=%fused_computation.9 | convolution fusion | flops 209166336 | bytes 12707328 | tf_op jit(solution)/shard_map/ntd,npd->ntp/dot_general | solution.py:44
  333.5 0.1 copy.32
  333.6 0.5 broadcast.518
  334.1 1.0 reduce.8
  335.1 0.2 reshape.533
  335.3 0.1 reduce_max.28
  335.4 0.1 copy.31
  335.4 0.7 pad_maximum_fusion
  336.2 0.0 all-reduce.2.cloned.1.call-update
  336.2 44.7 %all-reduce.2.cloned.1.call-done = f32[784,32]{0,1:T(8,128)} async-done(((f32[784,32]{0,1:T(8,128)}), f32[784,32]{0,1:T(8,128)}) %all-reduce.2.cloned.1.call-update) | async-done | bytes 100368 | tf_op jit(solution)/shard_map/pmax | solution.py:49
  381.0 1.0 slice_reduce_fusion
  382.0 0.7 div.94
  382.7 12.9 %all-to-all-start.1 = ((f32[64,1,12]{2,1,0:T(1,128)}), f32[64,1,12]{2,1,0:T(1,128)S(1)}, u32[]{:S(2)}, u32[]{:S(2)}) async-start(f32[64,1,12]{2,1,0:T(1,128)} %bitcast.9), calls=%async_computation.1 | async-start | bytes 65536 | tf_op jit(solution)/shard_map/all_to_all | solution.py:53
  395.6 0.1 gather.43
  395.7 0.1 reduce_sum.23
  395.7 0.7 slice.37
  396.5 0.7 copy.35
  397.1 7.7 %all-to-all-done.1 = f32[64,1,12]{2,1,0:T(1,128)S(1)} async-done(((f32[64,1,12]{2,1,0:T(1,128)}), f32[64,1,12]{2,1,0:T(1,128)S(1)}, u32[]{:S(2)}, u32[]{:S(2)}) %all-to-all-start.1) | async-done | bytes 3104 | tf_op jit(solution)/shard_map/all_to_all | solution.py:53
  404.9 0.5 broadcast.515
  405.4 0.7 reduce.7
  406.1 0.1 reshape.449
  406.2 1.4 gather_fusion.5
  407.6 0.1 gather.47
  407.7 0.6 and_select_fusion.2
  (32 shorter events, 0.3 us)
Async XLA Ops:
  7.2 280.2 %copy-start = (bf16[256,32,128]{2,1,0:T(8,128)(2,1)S(1)}, bf16[256,32,128]{2,1,0:T(8,128)(2,1)}, u32[]{:S(2)}) copy-start(bf16[256,32,128]{2,1,0:T(8,128)(2,1)} %param.8) | copy-start | bytes 6291460
  7.2 62.1 %copy-start.1 = (s32[16384]{0:T(1024)S(1)}, s32[16384]{0:T(1024)}, u32[]{:S(2)}) copy-start(s32[16384]{0:T(1024)} %param.10) | copy-start | bytes 196612
  7.2 285.1 %all-gather.2.cloned.1.call-start = ((), (), s32[]{:S(2)}) async-start(), calls=%async_computation.2 | async-start | bytes 8519680 | tf_op jit(solution)/shard_map/all_gather | solution.py:20
  69.0 90.8 %copy-start.4 = (s32[64,3]{0,1:T(4,128)}, s32[64,3]{0,1:T(4,128)S(1)}, u32[]{:S(2)}) copy-start(s32[64,3]{0,1:T(4,128)S(1)} %reduce-window.19) | copy-start | bytes 2308
  69.2 213.1 %copy-start.2 = (s32[256]{0:T(256)S(1)}, s32[256]{0:T(256)}, u32[]{:S(2)}) copy-start(s32[256]{0:T(256)} %param.9) | copy-start | bytes 3076
  287.3 4.6 %slice-start = ((s32[64,3]{0,1:T(4,128)}), s32[64,2]{0,1:T(2,128)S(1)}, s32[]{:S(2)}) async-start(s32[64,3]{0,1:T(4,128)} %copy-done.4), calls=%async_computation.4 | async-start | bytes 2048 | tf_op jit(solution)/shard_map/slice.5
  287.4 4.9 %copy-start.5 = (bf16[768,128]{1,0:T(8,128)(2,1)S(1)}, bf16[768,128]{1,0:T(8,128)(2,1)}, u32[]{:S(2)}) copy-start(bf16[768,128]{1,0:T(8,128)(2,1)} %param.7) | copy-start | bytes 589828
  310.4 23.2 %all-to-all-start = ((f32[64,1,512]{2,1,0:T(1,128)}), f32[64,1,512]{2,1,0:T(1,128)S(1)}, u32[]{:S(2)}, u32[]{:S(2)}) async-start(f32[64,1,512]{2,1,0:T(1,128)} %reshape.532), calls=%async_computation | async-start | bytes 262144 | tf_op jit(solution)/shard_map/all_to_all | solution.py:25
  316.8 64.1 %all-reduce.2.cloned.1.call-start = ((), (), s32[]{:S(2)}) async-start(), calls=%async_computation.3 | async-start | bytes 229376 | tf_op jit(solution)/shard_map/pmax | solution.py:49
  325.2 82.5 %copy-start.3 = (s32[16,16]{1,0:T(8,128)S(1)}, s32[16,16]{1,0:T(8,128)}, u32[]{:S(2)}) copy-start(s32[16,16]{1,0:T(8,128)} %param.11) | copy-start | bytes 3076
  382.7 22.2 %all-to-all-start.1 = ((f32[64,1,12]{2,1,0:T(1,128)}), f32[64,1,12]{2,1,0:T(1,128)S(1)}, u32[]{:S(2)}, u32[]{:S(2)}) async-start(f32[64,1,12]{2,1,0:T(1,128)} %bitcast.9), calls=%async_computation.1 | async-start | bytes 65536 | tf_op jit(solution)/shard_map/all_to_all | solution.py:53
Sparse Core Ops, SparseCore 0:
  10.8 87.3 all-gather.1
  336.3 44.5 all-reduce.1
where the time goes:
time: 416 us; the launch traced here: 415 us
  local copies, waits for them, and re-layouts  241 us (58%)
  blocking collectives  55.1 us (13%)
  waiting for transfers between devices  53.2 us (13%)
  matrix products  25.3 us (6%)
  starting transfers between devices  19.4 us (5%)
  between operations  14.4 us (3%)
  other arithmetic  6.63 us (2%)
    gather x1, local copies, waits for them, and re-layouts, per_device(): all_rows = jnp.take(passage_row, cand_block.reshape(-1), axis=0)  90.5 us
    scatter x1, local copies, waits for them, and re-layouts, per_device(): slot_table = jnp.zeros((shard_total * capacity,), jnp.int32).at[places].s...  60.5 us
    scatter x1, local copies, waits for them, and re-layouts, per_device(): jnp.zeros((shard_total * capacity,), jnp.int32).at[places]  60.3 us
    all_gather x1, blocking collectives, per_device(): cand_block = lax.all_gather(candidates, 'shard', axis=0, tiled=True)  55.1 us
    pmax x1, waiting for transfers between devices, per_device(): lax.pmax(jnp.concatenate([shard_best, partial_value], axis=0), 'cent')  44.7 us
    dot_general x1, matrix products, per_device(): jnp.einsum('rd,cd->rc', flattened, centroids, preferred_element_type=jnp....  17 us
    all_to_all x1, starting transfers between devices, per_device(): lax.all_to_all(pair_scores, 'shard', split_axis=0, concat_axis=0, tiled=T...  12.9 us
  transfers between devices with their start and end apart: 4, of which 2 were waited for; matrix products, arithmetic and copies ran while one was open for 60% of the time, Pallas kernels for 0%

commit v1 on v0

--- a/solution.py
+++ b/solution.py
@@ -4,6 +4,12 @@
 from jax.sharding import PartitionSpec as P
 
 masked_score = -1e30
+positions_rest = lambda local_block, row_axis: jnp.concatenate(
+    lax.all_to_all(
+        jnp.stack([local_block for _ in range(lax.axis_size(row_axis))]), row_axis, 0, 0
+    ),
+    axis=0,
+)
 
 
 def per_device(queries, centroids, passages, lengths, passage_row, candidates):
@@ -18,7 +24,7 @@
     pairs_here = query_count * per_query
     my_shard = lax.axis_index("shard")
     query_block = lax.all_gather(queries, "shard", axis=0, tiled=True)
-    cand_block = lax.all_gather(candidates, "shard", axis=0, tiled=True)
+    cand_block = positions_rest(candidates, "shard")
     flattened = query_block.reshape(-1, feature_width)
     scored = jnp.einsum("rd,cd->rc", flattened, centroids, preferred_element_type=jnp.float32)
     local_best = jnp.max(scored, axis=1).reshape(shard_total, query_count, query_tokens)

time: 416 us -> 381 us (0.916)
  blocking collectives: 55.1 us -> 0 us
  starting transfers between devices: 19.4 us -> 32.3 us
  waiting for transfers between devices: 53.2 us -> 57.4 us
    all_gather x1 -> x0, blocking collectives: 55.1 us -> none  [per_device(): cand_block = lax.all_gather(candidates, 'shard', axis=0, tiled=True)]
    all_to_all x0 -> x1, starting transfers between devices: none -> 13.1 us  [lax.all_to_all(jnp.stack([local_block for _ in range(lax.axis_size(row_ax...]
  transfers between devices with their start and end apart: 4 -> 5, of which waited for: 2 -> 3; matrix products, arithmetic and copies ran while one was open for 60% -> 66% of each run, Pallas kernels for 0% -> 0%
where the time goes in v1:
time: 381 us; the launch traced here: 380 us
  local copies, waits for them, and re-layouts  243 us (64%)
  waiting for transfers between devices  57.4 us (15%)
  starting transfers between devices  32.3 us (8%)
  matrix products  25.3 us (7%)
  between operations  14.4 us (4%)
  other arithmetic  7.43 us (2%)
    gather x1, local copies, waits for them, and re-layouts, per_device(): all_rows = jnp.take(passage_row, cand_block.reshape(-1), axis=0)  90.5 us
    scatter x1, local copies, waits for them, and re-layouts, per_device(): slot_table = jnp.zeros((shard_total * capacity,), jnp.int32).at[places].s...  60.5 us
    scatter x1, local copies, waits for them, and re-layouts, per_device(): jnp.zeros((shard_total * capacity,), jnp.int32).at[places]  60.3 us
    pmax x1, waiting for transfers between devices, per_device(): lax.pmax(jnp.concatenate([shard_best, partial_value], axis=0), 'cent')  44.7 us
    dot_general x1, matrix products, per_device(): jnp.einsum('rd,cd->rc', flattened, centroids, preferred_element_type=jnp....  17 us
    all_to_all x1, starting transfers between devices, lax.all_to_all(jnp.stack([local_block for _ in range(lax.axis_size(row_ax...  13.1 us
    all_to_all x1, starting transfers between devices, per_device(): lax.all_to_all(pair_scores, 'shard', split_axis=0, concat_axis=0, tiled=T...  12.9 us
    gather x1, local copies, waits for them, and re-layouts, per_device(): asked = jnp.take(query_block, query_table, axis=0)  8.3 us
  transfers between devices with their start and end apart: 5, of which 3 were waited for; matrix products, arithmetic and copies ran while one was open for 66% of the time, Pallas kernels for 0%

profile of v1, /device:TPU:1, one launch (start us, length us, event | category | flops | bytes accessed | tf_op | source)
XLA Modules:
  0.0 380.3 jit_solution(4466139559782979723)
XLA Ops:
  7.2 0.0 all-gather.2.cloned.1.call-start
  7.2 0.7 all-gather.2.cloned.1.call-update
  7.9 0.7 stack.2
  8.7 0.9 reshape.524
  9.5 13.1 %all-to-all-start.1 = ((s32[64,1,256]{2,1,0:T(1,128)}), s32[64,1,256]{2,1,0:T(1,128)S(1)}, u32[]{:S(2)}, u32[]{:S(2)}) async-start(s32[64,1,256]{2,1,0:T(1,128)} %reshape.524), calls=%async_computation.1 | async-start | bytes 131072 | tf_op jit(solution)/shard_map/all_to_all | solution.py:8
  22.7 0.8 reshape.437
  23.5 0.8 reshape.439
  24.2 0.8 reshape.438
  25.0 2.1 gather_fusion.4
  27.1 0.6 reduce-window.16
  27.8 0.2 slice_reduce_fusion.1
  28.0 0.1 broadcast_bitcast_fusion
  28.1 0.1 copy.41
  28.2 0.1 fusion.19
  28.3 4.2 %all-to-all-done.1 = s32[64,1,256]{2,1,0:T(1,128)S(1)} async-done(((s32[64,1,256]{2,1,0:T(1,128)}), s32[64,1,256]{2,1,0:T(1,128)S(1)}, u32[]{:S(2)}, u32[]{:S(2)}) %all-to-all-start.1) | async-done | bytes 65568 | tf_op jit(solution)/shard_map/all_to_all | solution.py:8
  32.4 0.5 broadcast.520
  32.9 0.8 reduce.8
  33.7 0.2 reshape.525
  33.9 0.2 reshape_reshape.7
  34.2 0.2 reshape_reshape.9
  34.4 0.3 copy.29
  34.6 0.1 compare_select_fusion.1
  34.8 90.5 %gather_fusion = s32[16384]{0:T(1024)S(1)} fusion(s32[16384]{0:T(1024)S(1)} %copy-done.1, s32[16384]{0:T(1024)S(1)} %broadcast_clamp_fusion), kind=kCustom, calls=%fused_computation | custom fusion | bytes 196608 | tf_op jit(solution)/shard_map/jit(_take)/gather | solution.py:33
  125.3 0.1 copy.30
  125.4 0.1 fusion.23
  125.5 0.6 reduce-window.14
  126.1 0.2 slice_reduce_fusion.2
  126.3 0.1 broadcast_add_fusion
  126.4 0.1 copy.34
  126.5 0.5 compare_select_fusion
  127.0 60.3 %scatter_custom_fusion.1 = s32[768]{0:T(1024)S(1)} fusion(s32[16384]{0:T(1024)S(1)} %bitcast.51, s32[16384]{0:T(1024)S(1)} %add_select_fusion, s32[]{:T(128)} %constant.143.clone.1), kind=kCustom, calls=%fused_computation.97 | custom fusion | bytes 3076 | tf_op jit(solution)/shard_map/scatter | solution.py:46
  187.4 60.5 %scatter_custom_fusion = s32[768]{0:T(1024)S(1)} fusion(s32[16384]{0:T(1024)S(1)} %bitcast.52, s32[16384]{0:T(1024)S(1)} %add_select_fusion.1, s32[]{:T(128)} %constant.143.clone.1), kind=kCustom, calls=%fused_computation.99 | custom fusion | bytes 3076 | tf_op jit(solution)/shard_map/scatter | solution.py:43
  247.9 5.0 %gather_fusion.1 = s32[768]{0:T(1024)S(1)} fusion(s32[256]{0:T(256)S(1)} %copy-done.2, s32[1024]{0:T(1024)S(1)} %pad_clamp_fusion.3), kind=kCustom, calls=%fused_computation.1 | custom fusion | bytes 9216 | tf_op jit(solution)/shard_map/jit(_take)/gather | solution.py:52
  252.9 4.5 %gather_fusion.3 = bf16[768,32,128]{2,1,0:T(8,128)(2,1)} fusion(bf16[256,32,128]{2,1,0:T(8,128)(2,1)S(1)} %copy-done, s32[1024]{0:T(1024)S(1)} %pad_clamp_fusion.3), kind=kCustom, calls=%fused_computation.3 | custom fusion | bytes 12585984 | tf_op jit(solution)/shard_map/jit(_take)/gather | solution.py:49
  257.5 0.2 broadcast_compare_fusion
  257.7 17.0 %convolution_reduce_fusion = f32[32768]{0:T(1024)S(1)} fusion(bf16[32768,128]{1,0:T(8,128)(2,1)} %bitcast.44, bf16[768,128]{1,0:T(8,128)(2,1)S(1)} %copy-done.4), kind=kOutput, calls=%fused_computation.8 | convolution fusion | flops 6467584000 | bytes 8716288 | tf_op jit(solution)/shard_map/rd,cd->rc/dot_general | solution.py:29
  274.7 0.2 reshape.435
  274.9 0.9 reshape.526
  275.8 6.2 %all-to-all-start = ((f32[64,1,512]{2,1,0:T(1,128)}), f32[64,1,512]{2,1,0:T(1,128)S(1)}, u32[]{:S(2)}, u32[]{:S(2)}) async-start(f32[64,1,512]{2,1,0:T(1,128)} %reshape.526), calls=%async_computation | async-start | bytes 262144 | tf_op jit(solution)/shard_map/all_to_all | solution.py:31
  282.0 0.0 all-reduce.2.cloned.1.call-start
  282.0 8.3 %gather_fusion.2 = bf16[768,32,128]{2,1,0:T(8,128)(2,1)} fusion(bf16[1024,32,128]{2,1,0:T(8,128)(2,1)} %all-gather.2.cloned.1.call-done, s32[1024]{0:T(1024)S(1)} %pad_clamp_fusion.2), kind=kCustom, calls=%fused_computation.2 | custom fusion | bytes 12585984 | tf_op jit(solution)/shard_map/jit(_take)/gather | solution.py:48
  290.3 8.3 %select_reduce_fusion = f32[768,32]{1,0:T(8,128)S(1)} fusion(pred[768,32]{1,0:T(8,128)(4,1)S(1)} %broadcast_compare_fusion, bf16[768,32,128]{2,1,0:T(8,128)(2,1)} %gather_fusion.3, pred[768]{0:T(1024)(128)(4,1)S(1)} %get-tuple-element.9, bf16[768,32,128]{2,1,0:T(8,128)(2,1)} %gather_fusion.2, pred[768]{0:T(1024)(128)(4,1)S(1)} %compare_and_fusion), kind=kOutput, calls=%fused_computation.9 | convolution fusion | flops 209166336 | bytes 12707328 | tf_op jit(solution)/shard_map/ntd,npd->ntp/dot_general | solution.py:50
  298.6 0.1 copy.36
  298.8 0.5 broadcast.521
  299.3 1.0 reduce.9
  300.2 0.2 reshape.527
  300.4 0.1 reduce_max.28
  300.5 0.1 copy.35
  300.6 0.7 pad_maximum_fusion
  301.4 44.7 %all-reduce.2.cloned.1.call-done = f32[784,32]{0,1:T(8,128)} async-done(((f32[784,32]{0,1:T(8,128)}), f32[784,32]{0,1:T(8,128)}) %all-reduce.2.cloned.1.call-update) | async-done | bytes 100368 | tf_op jit(solution)/shard_map/pmax | solution.py:55
  346.1 1.0 slice_reduce_fusion
  347.1 0.7 div.94
  347.8 12.9 %all-to-all-start.2 = ((f32[64,1,12]{2,1,0:T(1,128)}), f32[64,1,12]{2,1,0:T(1,128)S(1)}, u32[]{:S(2)}, u32[]{:S(2)}) async-start(f32[64,1,12]{2,1,0:T(1,128)} %bitcast.10), calls=%async_computation.2 | async-start | bytes 65536 | tf_op jit(solution)/shard_map/all_to_all | solution.py:59
  360.7 0.1 gather.43
  360.8 0.1 reduce_sum.23
  360.9 0.7 slice.37
  361.6 0.7 copy.39
  362.3 7.7 %all-to-all-done.2 = f32[64,1,12]{2,1,0:T(1,128)S(1)} async-done(((f32[64,1,12]{2,1,0:T(1,128)}), f32[64,1,12]{2,1,0:T(1,128)S(1)}, u32[]{:S(2)}, u32[]{:S(2)}) %all-to-all-start.2) | async-done | bytes 3104 | tf_op jit(solution)/shard_map/all_to_all | solution.py:59
  370.0 0.5 broadcast.517
  370.5 0.7 reduce.7
  371.3 0.1 reshape.441
  371.4 1.4 gather_fusion.5
  372.8 0.1 gather.47
  372.8 0.6 and_select_fusion.2
  (36 shorter events, 0.3 us)
Async XLA Ops:
  7.2 245.7 %copy-start = (bf16[256,32,128]{2,1,0:T(8,128)(2,1)S(1)}, bf16[256,32,128]{2,1,0:T(8,128)(2,1)}, u32[]{:S(2)}) copy-start(bf16[256,32,128]{2,1,0:T(8,128)(2,1)} %param.8) | copy-start | bytes 6291460
  7.2 27.6 %copy-start.1 = (s32[16384]{0:T(1024)S(1)}, s32[16384]{0:T(1024)}, u32[]{:S(2)}) copy-start(s32[16384]{0:T(1024)} %param.10) | copy-start | bytes 196612
  7.2 250.5 %all-gather.2.cloned.1.call-start = ((), (), s32[]{:S(2)}) async-start(), calls=%async_computation.3 | async-start | bytes 8519680 | tf_op jit(solution)/shard_map/all_gather | solution.py:26
  9.5 22.9 %all-to-all-start.1 = ((s32[64,1,256]{2,1,0:T(1,128)}), s32[64,1,256]{2,1,0:T(1,128)S(1)}, u32[]{:S(2)}, u32[]{:S(2)}) async-start(s32[64,1,256]{2,1,0:T(1,128)} %reshape.524), calls=%async_computation.1 | async-start | bytes 131072 | tf_op jit(solution)/shard_map/all_to_all | solution.py:8
  34.7 213.1 %copy-start.2 = (s32[256]{0:T(256)S(1)}, s32[256]{0:T(256)}, u32[]{:S(2)}) copy-start(s32[256]{0:T(256)} %param.9) | copy-start | bytes 3076
  252.9 4.8 %copy-start.4 = (bf16[768,128]{1,0:T(8,128)(2,1)S(1)}, bf16[768,128]{1,0:T(8,128)(2,1)}, u32[]{:S(2)}) copy-start(bf16[768,128]{1,0:T(8,128)(2,1)} %param.7) | copy-start | bytes 589828
  275.8 23.0 %all-to-all-start = ((f32[64,1,512]{2,1,0:T(1,128)}), f32[64,1,512]{2,1,0:T(1,128)S(1)}, u32[]{:S(2)}, u32[]{:S(2)}) async-start(f32[64,1,512]{2,1,0:T(1,128)} %reshape.526), calls=%async_computation | async-start | bytes 262144 | tf_op jit(solution)/shard_map/all_to_all | solution.py:31
  282.0 64.1 %all-reduce.2.cloned.1.call-start = ((), (), s32[]{:S(2)}) async-start(), calls=%async_computation.4 | async-start | bytes 229376 | tf_op jit(solution)/shard_map/pmax | solution.py:55
  290.3 82.5 %copy-start.3 = (s32[16,16]{1,0:T(8,128)S(1)}, s32[16,16]{1,0:T(8,128)}, u32[]{:S(2)}) copy-start(s32[16,16]{1,0:T(8,128)} %param.11) | copy-start | bytes 3076
  347.8 22.2 %all-to-all-start.2 = ((f32[64,1,12]{2,1,0:T(1,128)}), f32[64,1,12]{2,1,0:T(1,128)S(1)}, u32[]{:S(2)}, u32[]{:S(2)}) async-start(f32[64,1,12]{2,1,0:T(1,128)} %bitcast.10), calls=%async_computation.2 | async-start | bytes 65536 | tf_op jit(solution)/shard_map/all_to_all | solution.py:59
Sparse Core Ops, SparseCore 0:
  10.8 87.2 all-gather.1
  301.5 44.5 all-reduce.1
